TPU v7x, 256 devices: a whole 4x4x8 slice. The times are simulated.
256 devices in a mesh: batch: 8 (over z), replica: 32 (over y, x, core).
Axes of the slice: x: 4, y: 4, z: 8, core: 2. Of those that a mesh axis runs over, the one named last changes fastest.
Arguments:
- patches: bfloat16 [32, 64, 64, 1024], P('replica', 'batch'), may hold values from -6 to 6
- visible_order: int32 [32, 64, 64], P('replica', 'batch'), may hold values from 0 to 63, each once within a row
- visible_counts: int32 [32, 64], P('replica'), may hold values from 1 to 32, as said below
- dest_rows: int32 [32, 64], P('replica'), may hold values from 0 to 1023, as said below
- qkv_weight: bfloat16 [1024, 3072], P('replica')
- out_weight: bfloat16 [1024, 1024], P('replica'), may hold values from -0.1875 to 0.1875
- norm_gain: bfloat16 [1024], P('replica'), may hold values from 0.5 to 1.5
- upstream: bfloat16 [32, 1024, 1024], P('replica', 'batch'), may hold values from -6 to 6
Outputs:
- layer_out: bfloat16 [32, 1024, 1024], P('replica', 'batch')
- d_packed: bfloat16 [32, 1024, 1024], P('replica', 'batch')
- grad_qkv: float32 [1024, 3072], P('replica')
- grad_out: float32 [1024, 1024], P('replica')
- grad_gain: float32 [1024], P('replica')
Inputs may be any that keep to these rules, and one draw needn't show every extreme that they name: `visible_counts`: in every replica index, each batch index b packs exactly 128 rows: the volumes with dest_rows // 128 == b, one from every device of the batch axis, in order of that device's batch index, without gaps; one of them has 32 visible patches. `dest_rows`: the 8 volumes of one device go to 8 different batch indices; a volume's rows never cross a multiple of 128.
All inputs are finite; a program needn't handle non-finite values.
Results may differ from a plain program's by a relative error of at most 0.033.
Values may be sent and summed in bfloat16 or wider, within the bound.
No kernel may reach another device: no remote copies, remote signals or barrier semaphores. Data moves between devices by JAX's collectives and lax.ppermute only.
A program may use at most 128 MiB of HBM per device.

v0:
```python
import jax
import jax.numpy as jnp
from jax import lax
from jax.sharding import PartitionSpec as P

HEADS = 16
MAXVIS = 32
MEANVIS = 16
EPS = 1e-06
NEG = -1e30


def layer_core(tokens, upward, allowed, wqkv, wout, gain):
    groups, length, width = tokens.shape
    rows = groups * length
    head_dim = width // HEADS
    scale = head_dim ** (-0.5)
    x32 = tokens.astype(jnp.float32).reshape(rows, width)
    row_average = jnp.mean(x32, axis=1, keepdims=True)
    centered_rows = x32 - row_average
    inverse_deviation = lax.rsqrt(
        jnp.mean(centered_rows * centered_rows, axis=1, keepdims=True) + EPS
    )
    standardized_rows = centered_rows * inverse_deviation
    gain_float32 = gain.astype(jnp.float32)
    layernorm_output = (standardized_rows * gain_float32).astype(jnp.bfloat16)
    qkv = jnp.dot(layernorm_output, wqkv, preferred_element_type=jnp.float32).astype(jnp.bfloat16)
    query = qkv[:, :width].reshape(groups, length, HEADS, head_dim)
    keys = qkv[:, width : 2 * width].reshape(groups, length, HEADS, head_dim)
    values = qkv[:, 2 * width :].reshape(groups, length, HEADS, head_dim)
    scores = jnp.einsum("gqhd,gkhd->ghqk", query, keys, preferred_element_type=jnp.float32) * scale
    scores = jnp.where(allowed[:, None], scores, NEG)
    top = jnp.max(scores, axis=-1, keepdims=True)
    expd = jnp.exp(scores - top)
    probs = expd / jnp.sum(expd, axis=-1, keepdims=True)
    weights = probs.astype(jnp.bfloat16)
    context = (
        jnp.einsum("ghqk,gkhd->gqhd", weights, values, preferred_element_type=jnp.float32)
        .astype(jnp.bfloat16)
        .reshape(rows, width)
    )
    result = (x32 + jnp.dot(context, wout, preferred_element_type=jnp.float32)).astype(jnp.bfloat16)
    up_rows = upward.reshape(rows, width)
    d_context = lax.dot_general(
        up_rows, wout, (((1,), (1,)), ((), ())), preferred_element_type=jnp.float32
    ).astype(jnp.bfloat16)
    d_context = d_context.reshape(groups, length, HEADS, head_dim)
    d_values = jnp.einsum(
        "ghqk,gqhd->gkhd", weights, d_context, preferred_element_type=jnp.float32
    ).astype(jnp.bfloat16)
    d_weights = jnp.einsum("gqhd,gkhd->ghqk", d_context, values, preferred_element_type=jnp.float32)
    d_scores = (
        probs * (d_weights - jnp.sum(d_weights * probs, axis=-1, keepdims=True)) * scale
    ).astype(jnp.bfloat16)
    d_query = jnp.einsum(
        "ghqk,gkhd->gqhd", d_scores, keys, preferred_element_type=jnp.float32
    ).astype(jnp.bfloat16)
    d_keys = jnp.einsum(
        "ghqk,gqhd->gkhd", d_scores, query, preferred_element_type=jnp.float32
    ).astype(jnp.bfloat16)
    d_qkv = jnp.concatenate(
        [d_query.reshape(rows, width), d_keys.reshape(rows, width), d_values.reshape(rows, width)],
        axis=1,
    )
    layernorm_gradient = lax.dot_general(
        d_qkv, wqkv, (((1,), (1,)), ((), ())), preferred_element_type=jnp.float32
    )
    gain_products = jnp.sum(layernorm_gradient * standardized_rows, axis=0)
    normalized_gradient = layernorm_gradient * gain_float32
    input_gradient = inverse_deviation * (
        normalized_gradient
        - jnp.mean(normalized_gradient, axis=1, keepdims=True)
        - standardized_rows
        * jnp.mean(normalized_gradient * standardized_rows, axis=1, keepdims=True)
    )
    d_tokens = (up_rows.astype(jnp.float32) + input_gradient).astype(jnp.bfloat16)
    return (
        result.reshape(tokens.shape),
        d_tokens.reshape(tokens.shape),
        layernorm_output,
        context,
        d_qkv,
        up_rows,
        gain_products,
    )


def left_product(left, right):
    return lax.dot_general(
        left, right, (((0,), (0,)), ((), ())), preferred_element_type=jnp.float32
    )


def on_device(
    patches, visible_order, visible_counts, dest_rows, qkv_weight, out_weight, norm_gain, upstream
):
    qkv_cols = qkv_weight.shape[1]
    out_cols = out_weight.shape[1]
    gain_block = jnp.broadcast_to(norm_gain[:, None], (norm_gain.shape[0], 128))
    gathered = lax.all_gather(
        jnp.concatenate([qkv_weight, out_weight, gain_block], axis=1), "replica", axis=0, tiled=True
    )
    wqkv = gathered[:, :qkv_cols]
    wout = gathered[:, qkv_cols : qkv_cols + out_cols]
    gain = gathered[:, qkv_cols + out_cols]
    batches = lax.axis_size("batch")
    me_index = lax.axis_index("batch")
    cap = MEANVIS * batches
    width = wout.shape[1]
    slot = jnp.arange(MAXVIS, dtype=jnp.int32)
    sources = jnp.arange(batches, dtype=jnp.int32)
    counts_all = visible_counts[0].reshape(batches, batches)
    rows_all = dest_rows[0].reshape(batches, batches)
    mine = rows_all // cap == me_index
    src_count = jnp.sum(jnp.where(mine, counts_all, 0), axis=1)
    src_start = jnp.sum(jnp.where(mine, rows_all % cap, 0), axis=1)
    position = jnp.arange(cap, dtype=jnp.int32)
    hit = (position[:, None] >= src_start[None, :]) & (
        position[:, None] < (src_start + src_count)[None, :]
    )
    segment = jnp.sum(jnp.where(hit, sources[None, :], 0), axis=1)
    inside = jnp.sum(jnp.where(hit, position[:, None] - src_start[None, :], 0), axis=1)
    flat_rows = segment * MAXVIS + inside
    my_targets = jnp.take(rows_all, me_index, axis=0) // cap
    to_target = jnp.sum(
        jnp.where(my_targets[None, :] == sources[:, None], sources[None, :], 0), axis=1
    )
    my_counts = jnp.take(counts_all, me_index, axis=0)
    local_rows = jnp.take_along_axis(patches[0], visible_order[0, :, :MAXVIS, None], axis=1)
    live = slot[None, :] < src_count[:, None]
    pick = jnp.clip(src_start[:, None] + slot[None, :], 0, cap - 1)
    fetched = jnp.take(upstream[0], pick.reshape(-1), axis=0).reshape(batches, MAXVIS, width)
    backward_rows = jnp.where(live[..., None], fetched, jnp.zeros_like(fetched))
    returned = lax.all_to_all(backward_rows, "batch", split_axis=0, concat_axis=0, tiled=True)
    upward = jnp.take(returned, my_targets, axis=0)
    valid = slot[None, :] < my_counts[:, None]
    allowed = jnp.broadcast_to(valid[:, None, :], (batches, MAXVIS, MAXVIS))
    result, d_tokens, layernorm_output, context, d_qkv, up_rows, gain_products = layer_core(
        local_rows, upward, allowed, wqkv, wout, gain
    )
    came = lax.all_to_all(
        jnp.take(jnp.concatenate([result, d_tokens], axis=-1), to_target, axis=0),
        "batch",
        split_axis=0,
        concat_axis=0,
        tiled=True,
    )
    came_out = came[..., :width]
    came_grad = came[..., width:]
    layer_out = jnp.take(came_out.reshape(batches * MAXVIS, width), flat_rows, axis=0)
    d_packed = jnp.take(came_grad.reshape(batches * MAXVIS, width), flat_rows, axis=0)
    partial = jnp.concatenate(
        [
            left_product(layernorm_output, d_qkv).astype(jnp.bfloat16),
            left_product(context, up_rows).astype(jnp.bfloat16),
            jnp.broadcast_to(gain_products.astype(jnp.bfloat16)[:, None], (width, 128)),
        ],
        axis=1,
    )
    summed = lax.psum_scatter(partial, "replica", scatter_dimension=0, tiled=True)
    summed = lax.psum(summed, "batch").astype(jnp.float32)
    grad_q = summed[:, :qkv_cols]
    grad_o = summed[:, qkv_cols : qkv_cols + out_cols]
    grad_g = summed[:, qkv_cols + out_cols]
    return (layer_out[None], d_packed[None], grad_q, grad_o, grad_g)


def solution(mesh):
    placed = (
        P("replica", "batch", None, None),
        P("replica", "batch", None),
        P("replica", None),
        P("replica", None),
        P("replica", None),
        P("replica", None),
        P("replica"),
        P("replica", "batch", None),
    )
    return jax.shard_map(
        on_device,
        mesh=mesh,
        in_specs=placed,
        out_specs=(
            P("replica", "batch", None),
            P("replica", "batch", None),
            P("replica", None),
            P("replica", None),
            P("replica"),
        ),
        check_vma=False,
    )
```

profile of v0, /device:TPU:2, one launch (start us, length us, event | category | flops | bytes accessed | tf_op | source)
XLA Modules:
  0.0 334.6 jit_solution(9900112664250814567)
XLA Ops:
  8.1 1.7 pad_maximum_fusion.2
  10.3 1.3 reduce.13
  11.7 1.3 reduce.12
  13.5 1.2 gather_fusion
  14.7 1.0 select_select_fusion
  15.7 8.5 %all-to-all-start = ((bf16[8,32,1024]{2,1,0:T(8,128)(2,1)}), bf16[8,32,1024]{2,1,0:T(8,128)(2,1)S(1)}, u32[]{:S(2)}, u32[]{:S(2)}) async-start(bf16[8,32,1024]{2,1,0:T(8,128)(2,1)} %select_select_fusion), calls=%async_computation | async-start | bytes 1048576 | tf_op jit(solution)/shard_map/all_to_all | solution.py:134
  24.3 2.8 gather_fusion.3
  28.2 13.4 %all-to-all-done = bf16[8,32,1024]{2,1,0:T(8,128)(2,1)S(1)} async-done(((bf16[8,32,1024]{2,1,0:T(8,128)(2,1)}), bf16[8,32,1024]{2,1,0:T(8,128)(2,1)S(1)}, u32[]{:S(2)}, u32[]{:S(2)}) %all-to-all-start) | async-done | bytes 524320 | tf_op jit(solution)/shard_map/all_to_all | solution.py:134
  42.2 0.9 broadcast_select_fusion.1
  43.3 29.1 %all-gather.2.cloned.1.call-done = bf16[1024,4224]{1,0:T(8,128)(2,1)} async-done(((bf16[32,4224]{1,0:T(8,128)(2,1)}), bf16[1024,4224]{1,0:T(8,128)(2,1)}) %all-gather.2.cloned.1.call-update) | async-done | bytes 8650768 | tf_op jit(solution)/shard_map/all_gather | solution.py:100
  72.4 3.2 fusion.43
  75.6 1.8 reshape.307
  77.3 1.1 convert_reduce_fusion.1
  78.4 4.7 %fusion.6 = bf16[256,3072]{1,0:T(8,128)(2,1)S(1)} fusion(bf16[1024,4224]{1,0:T(8,128)(2,1)} %all-gather.2.cloned.1.call-done, f32[1024]{0:T(1024)S(1)} %convert_reduce_fusion.1, f32[256]{0:T(256)S(1)} %rsqrt.12, f32[256]{0:T(256)S(1)} %div.51, bf16[256,1024]{1,0:T(8,128)(2,1)S(1)} %gather_fusion.3, pred[256]{0:T(512)(128)(4,1)S(1)} %compare_and_fusion.4), kind=kOutput, calls=%fused_computation.14 | convolution fusion | flops 1612972032 | bytes 8395008 | tf_op jit(solution)/shard_map/dot_general | solution.py:27
  83.2 1.2 fusion.109
  84.4 2.5 reshape.302
  86.9 2.5 reshape.304
  89.4 2.5 reshape.303
  91.9 3.2 fusion.66
  95.1 4.1 %fusion.111 = (f32[8,16,32]{2,1,0:T(8,128)S(1)}, f32[8,16,32,32]{2,3,1,0:T(8,128)}) fusion(pred[8,32]{1,0:T(8,128)(4,1)S(1)} %iota_compare_fusion.3, bf16[8,32,16,64]{3,2,1,0:T(8,128)(2,1)} %reshape.304, bf16[8,32,16,64]{3,2,1,0:T(8,128)(2,1)} %reshape.303), kind=kOutput, calls=%fused_computation.155 | convolution fusion | flops 17301536 | bytes 1589504 | tf_op jit(solution)/shard_map/sub | solution.py:34
  99.2 5.8 %fusion.34 = bf16[8,32,16,64]{3,1,2,0:T(8,128)(2,1)} fusion(f32[8,16,32,32]{2,3,1,0:T(8,128)} %fusion.66, bf16[8,32,16,64]{3,2,1,0:T(8,128)(2,1)} %reshape.304, f32[8,16,32,32]{2,3,1,0:T(8,128)} %get-tuple-element.37, f32[8,16,32]{2,1,0:T(8,128)S(1)} %get-tuple-element.36), kind=kOutput, calls=%fused_computation.35 | convolution fusion | flops 17960992 | bytes 2113536 | tf_op jit(solution)/shard_map/ghqk,gkhd->gqhd/dot_general | solution.py:55
  104.9 5.6 %fusion.31 = bf16[8,32,16,64]{3,1,2,0:T(8,128)(2,1)} fusion(f32[8,16,32,32]{2,3,1,0:T(8,128)} %fusion.66, bf16[8,32,16,64]{3,2,1,0:T(8,128)(2,1)} %reshape.303, f32[8,16,32,32]{2,3,1,0:T(8,128)} %get-tuple-element.37, f32[8,16,32]{2,1,0:T(8,128)S(1)} %get-tuple-element.36), kind=kOutput, calls=%fused_computation.34 | convolution fusion | flops 17960992 | bytes 2113536 | tf_op jit(solution)/shard_map/ghqk,gqhd->gkhd/dot_general | solution.py:58
  110.6 3.2 fusion.30
  113.8 1.6 fusion.29
  115.8 1.5 reshape.308
  117.3 1.9 constant_dynamic-update-slice_fusion.2
  119.2 1.6 copy.50
  120.9 1.5 reshape.309
  122.4 1.6 copy.52
  124.1 1.5 reshape.310
  125.6 1.6 copy.43
  127.2 1.5 reshape.305
  128.7 1.9 constant_dynamic-update-slice_fusion.1
  130.7 1.9 constant_dynamic-update-slice_fusion
  132.6 3.5 %convolution_convert_fusion = bf16[1024,3072]{1,0:T(8,128)(2,1)S(1)} fusion(bf16[256,3072]{1,0:T(8,128)(2,1)} %constant_dynamic-update-slice_fusion, f32[1024]{0:T(1024)S(1)} %convert_reduce_fusion.1, f32[256]{0:T(256)S(1)} %rsqrt.12, f32[256]{0:T(256)S(1)} %div.51, bf16[256,1024]{1,0:T(8,128)(2,1)S(1)} %gather_fusion.3, pred[256]{0:T(512)(128)(4,1)S(1)} %compare_and_fusion.4), kind=kOutput, calls=%fused_computation.9 | convolution fusion | flops 1615331328 | bytes 8395008 | tf_op jit(solution)/shard_map/dot_general | solution.py:89
  136.1 1.0 convolution_convert_fusion.1
  137.5 5.8 %fusion.57 = (bf16[1024]{0:T(1024)(128)(2,1)S(1)}, f32[256]{0:T(256)S(1)}, f32[256]{0:T(256)S(1)}, f32[256,1024]{1,0:T(8,128)}) fusion(f32[256]{0:T(256)S(1)} %rsqrt.12, f32[256]{0:T(256)S(1)} %div.51, bf16[256,1024]{1,0:T(8,128)(2,1)S(1)} %gather_fusion.3, pred[256]{0:T(512)(128)(4,1)S(1)} %compare_and_fusion.4, f32[1024]{0:T(1024)S(1)} %convert_reduce_fusion.1, ...), kind=kOutput, calls=%fused_computation.53 | convolution fusion | flops 1613232640 | bytes 9447680 | tf_op jit(solution)/shard_map/dot_general | solution.py:65
  143.5 3.7 %pad_maximum_fusion = bf16[1024,4224]{1,0:T(8,128)(2,1)} fusion(bf16[1024,128]{1,0:T(8,128)(2,1)S(1)} %broadcast_in_dim.181, bf16[1024,1024]{1,0:T(8,128)(2,1)S(1)} %convolution_convert_fusion.1, bf16[1024,3072]{1,0:T(8,128)(2,1)S(1)} %convolution_convert_fusion), kind=kLoop, calls=%fused_computation.8 | loop fusion | flops 25952256 | bytes 17301504 | tf_op jit(solution)/shard_map/concatenate | solution.py:152
  147.5 1.7 fusion.56
  149.2 2.3 fusion.40
  152.3 1.2 broadcast_select_fusion
  153.4 7.0 %all-to-all-start.1 = ((bf16[8,32,2048]{2,1,0:T(8,128)(2,1)}), bf16[8,32,2048]{2,1,0:T(8,128)(2,1)S(1)}, u32[]{:S(2)}, u32[]{:S(2)}) async-start(bf16[8,32,2048]{2,1,0:T(8,128)(2,1)} %broadcast_select_fusion), calls=%async_computation.1 | async-start | bytes 2097152 | tf_op jit(solution)/shard_map/all_to_all | solution.py:141
  160.5 87.6 %reduce-scatter.2.cloned.1.call-done = bf16[32,4224]{1,0:T(8,128)(2,1)} async-done(((bf16[1024,4224]{1,0:T(8,128)(2,1)}), bf16[32,4224]{1,0:T(8,128)(2,1)}) %reduce-scatter.2.cloned.1.call-update) | async-done | bytes 270352 | tf_op jit(solution)/shard_map/reduce_scatter | solution.py:160
  249.9 0.9 select_bitcast_fusion
  250.8 72.4 %all-reduce.2.cloned.1.call-done = bf16[32,4224]{1,0:T(8,128)(2,1)} async-done(((bf16[32,4224]{1,0:T(8,128)(2,1)}), bf16[32,4224]{1,0:T(8,128)(2,1)}) %all-reduce.2.cloned.1.call-update) | async-done | bytes 270352 | tf_op jit(solution)/shard_map/psum | solution.py:161
  323.3 1.0 convert_element_type.105
  324.9 1.7 slice.75
  326.6 1.5 slice.76
  (72 shorter events, 8.4 us)
Async XLA Ops:
  7.2 17.1 %copy-start = (bf16[1,8,64,1024]{3,2,1,0:T(8,128)(2,1)S(1)}, bf16[1,8,64,1024]{3,2,1,0:T(8,128)(2,1)}, u32[]{:S(2)}) copy-start(bf16[1,8,64,1024]{3,2,1,0:T(8,128)(2,1)} %param.12) | copy-start | bytes 3145732
  7.2 6.3 %copy-start.1 = (bf16[1,128,1024]{2,1,0:T(8,128)(2,1)S(1)}, bf16[1,128,1024]{2,1,0:T(8,128)(2,1)}, u32[]{:S(2)}) copy-start(bf16[1,128,1024]{2,1,0:T(8,128)(2,1)} %param.19) | copy-start | bytes 786436
  7.2 65.2 %all-gather.2.cloned.1.call-start = ((), (), s32[]{:S(2)}) async-start(), calls=%async_computation.3 | async-start | bytes 8921088 | tf_op jit(solution)/shard_map/all_gather | solution.py:100
  14.6 9.6 %copy-start.7 = (s32[1,8,64]{2,1,0:T(8,128)S(1)}, s32[1,8,64]{2,1,0:T(8,128)}, u32[]{:S(2)}) copy-start(s32[1,8,64]{2,1,0:T(8,128)} %param.13) | copy-start | bytes 6148
  15.7 26.0 %all-to-all-start = ((bf16[8,32,1024]{2,1,0:T(8,128)(2,1)}), bf16[8,32,1024]{2,1,0:T(8,128)(2,1)S(1)}, u32[]{:S(2)}, u32[]{:S(2)}) async-start(bf16[8,32,1024]{2,1,0:T(8,128)(2,1)} %select_select_fusion), calls=%async_computation | async-start | bytes 1048576 | tf_op jit(solution)/shard_map/all_to_all | solution.py:134
  24.2 223.9 %reduce-scatter.2.cloned.1.call-start = ((), (), s32[]{:S(2)}) async-start(), calls=%async_computation.4 | async-start | bytes 8921088 | tf_op jit(solution)/shard_map/reduce_scatter | solution.py:160
  110.6 3.2 copy-start.2
  110.6 3.2 copy-start.8
  113.8 1.6 copy-start.6
  132.6 3.6 %copy-start.4 = (bf16[256,1024]{1,0:T(8,128)(2,1)S(1)}, bf16[256,1024]{1,0:T(8,128)(2,1)}, u32[]{:S(2)}) copy-start(bf16[256,1024]{1,0:T(8,128)(2,1)} %reshape.305) | copy-start | bytes 1572868
  132.6 3.6 %copy-start.5 = (bf16[8,32,1024]{2,1,0:T(8,128)(2,1)S(1)}, bf16[8,32,1024]{2,1,0:T(8,128)(2,1)}, u32[]{:S(2)}) copy-start(bf16[8,32,1024]{2,1,0:T(8,128)(2,1)} %broadcast_select_fusion.1) | copy-start | bytes 1572868
  136.1 1.4 copy-start.3
  153.4 94.7 %all-to-all-start.1 = ((bf16[8,32,2048]{2,1,0:T(8,128)(2,1)}), bf16[8,32,2048]{2,1,0:T(8,128)(2,1)S(1)}, u32[]{:S(2)}, u32[]{:S(2)}) async-start(bf16[8,32,2048]{2,1,0:T(8,128)(2,1)} %broadcast_select_fusion), calls=%async_computation.1 | async-start | bytes 2097152 | tf_op jit(solution)/shard_map/all_to_all | solution.py:141
  160.4 162.8 %all-reduce.2.cloned.1.call-start = ((), (), s32[]{:S(2)}) async-start(), calls=%async_computation.5 | async-start | bytes 540672 | tf_op jit(solution)/shard_map/psum | solution.py:161
Sparse Core Ops, SparseCore 0:
  11.1 61.2 all-gather.1
  147.3 100.6 reduce-scatter.1
  250.4 72.8 all-reduce.1
where the time goes:
time: 336 us; the launch traced here: 335 us
  waiting for transfers between devices  203 us (60%)
  matrix products  44 us (13%)
  local copies, waits for them, and re-layouts  41.1 us (12%)
  other arithmetic  17.3 us (5%)
  starting transfers between devices  15.6 us (5%)
  between operations  14.1 us (4%)
    reduce_scatter x1, waiting for transfers between devices, on_device(): lax.psum_scatter(partial, 'replica', scatter_dimension=0, tiled=True)  87.6 us
    psum x1, waiting for transfers between devices, on_device(): summed = lax.psum(summed, 'batch').astype(jnp.float32)  72.4 us
    all_gather x1, waiting for transfers between devices, on_device(): lax.all_gather(jnp.concatenate([qkv_weight, out_weight, gain_block], axis...  29.1 us
    all_to_all x1, waiting for transfers between devices, on_device(): lax.all_to_all(backward_rows, 'batch', split_axis=0, concat_axis=0, tiled...  13.4 us
    all_to_all x1, starting transfers between devices, on_device(): lax.all_to_all(backward_rows, 'batch', split_axis=0, concat_axis=0, tiled...  8.47 us
    all_to_all x1, starting transfers between devices, on_device(): lax.all_to_all(jnp.take(jnp.concatenate([result, d_tokens], axis=-1), to_...  7.02 us
  transfers between devices with their start and end apart: 5, of which 4 were waited for; matrix products, arithmetic and copies ran while one was open for 6% of the time, Pallas kernels for 0%

commit v1 on v0

--- a/solution.py
+++ b/solution.py
@@ -97,8 +97,17 @@
     qkv_cols = qkv_weight.shape[1]
     out_cols = out_weight.shape[1]
     gain_block = jnp.broadcast_to(norm_gain[:, None], (norm_gain.shape[0], 128))
-    gathered = lax.all_gather(
-        jnp.concatenate([qkv_weight, out_weight, gain_block], axis=1), "replica", axis=0, tiled=True
+    gathered = jnp.concatenate(
+        lax.all_to_all(
+            jnp.stack(
+                [jnp.concatenate([qkv_weight, out_weight, gain_block], axis=1)]
+                * lax.axis_size("replica")
+            ),
+            "replica",
+            0,
+            0,
+        ),
+        axis=0,
     )
     wqkv = gathered[:, :qkv_cols]
     wout = gathered[:, qkv_cols : qkv_cols + out_cols]

time: 336 us -> 410 us (1.22)
  waiting for transfers between devices: 203 us -> 277 us
  local copies, waits for them, and re-layouts: 41.1 us -> 35.5 us
  starting transfers between devices: 15.6 us -> 19.9 us
    all_to_all x0 -> x1, waiting for transfers between devices: none -> 96.8 us  [on_device(): lax.all_to_all(jnp.stack([jnp.concatenate([qkv_weight, out_weight, gain_b...]
    all_gather x1 -> x0, waiting for transfers between devices: 29.1 us -> none  [on_device(): lax.all_gather(jnp.concatenate([qkv_weight, out_weight, gain_block], axis...]
    all_to_all x0 -> x1, starting transfers between devices: none -> 7.8 us  [on_device(): lax.all_to_all(jnp.stack([jnp.concatenate([qkv_weight, out_weight, gain_b...]
  transfers between devices with their start and end apart: 5 -> 5, of which waited for: 4 -> 4; matrix products, arithmetic and copies ran while one was open for 6% -> 3% of each run, Pallas kernels for 0% -> 0%
where the time goes in v1:
time: 410 us; the launch traced here: 409 us
  waiting for transfers between devices  277 us (68%)
  matrix products  44.8 us (11%)
  local copies, waits for them, and re-layouts  35.5 us (9%)
  starting transfers between devices  19.9 us (5%)
  other arithmetic  17.2 us (4%)
  between operations  14.4 us (4%)
    all_to_all x1, waiting for transfers between devices, on_device(): lax.all_to_all(jnp.stack([jnp.concatenate([qkv_weight, out_weight, gain_b...  96.8 us
    reduce_scatter x1, waiting for transfers between devices, on_device(): lax.psum_scatter(partial, 'replica', scatter_dimension=0, tiled=True)  90.4 us
    psum x1, waiting for transfers between devices, on_device(): summed = lax.psum(summed, 'batch').astype(jnp.float32)  72.4 us
    all_to_all x1, waiting for transfers between devices, on_device(): lax.all_to_all(backward_rows, 'batch', split_axis=0, concat_axis=0, tiled...  17.4 us
    all_to_all x1, starting transfers between devices, on_device(): lax.all_to_all(backward_rows, 'batch', split_axis=0, concat_axis=0, tiled...  8.47 us
  transfers between devices with their start and end apart: 5, of which 4 were waited for; matrix products, arithmetic and copies ran while one was open for 3% of the time, Pallas kernels for 0%

profile of v1, /device:TPU:2, one launch (start us, length us, event | category | flops | bytes accessed | tf_op | source)
XLA Modules:
  0.0 408.8 jit_solution(18375787369652851128)
XLA Ops:
  7.7 1.3 reduce.13
  9.1 1.3 reduce.12
  10.9 2.5 gather_fusion
  13.5 0.9 select_select_fusion
  14.4 8.5 %all-to-all-start.1 = ((bf16[8,32,1024]{2,1,0:T(8,128)(2,1)}), bf16[8,32,1024]{2,1,0:T(8,128)(2,1)S(1)}, u32[]{:S(2)}, u32[]{:S(2)}) async-start(bf16[8,32,1024]{2,1,0:T(8,128)(2,1)} %select_select_fusion), calls=%async_computation.1 | async-start | bytes 1048576 | tf_op jit(solution)/shard_map/all_to_all | solution.py:143
  23.0 17.4 %all-to-all-done.1 = bf16[8,32,1024]{2,1,0:T(8,128)(2,1)S(1)} async-done(((bf16[8,32,1024]{2,1,0:T(8,128)(2,1)}), bf16[8,32,1024]{2,1,0:T(8,128)(2,1)S(1)}, u32[]{:S(2)}, u32[]{:S(2)}) %all-to-all-start.1) | async-done | bytes 524320 | tf_op jit(solution)/shard_map/all_to_all | solution.py:143
  40.4 3.9 stack.2
  44.3 7.8 %all-to-all-start = ((bf16[32,32,4224]{2,1,0:T(8,128)(2,1)}), bf16[32,32,4224]{2,1,0:T(8,128)(2,1)}, u32[]{:S(2)}, u32[]{:S(2)}) async-start(bf16[32,32,4224]{2,1,0:T(8,128)(2,1)} %stack.2), calls=%async_computation | async-start | bytes 17301504 | tf_op jit(solution)/shard_map/all_to_all | solution.py:101
  52.2 2.8 gather_fusion.3
  56.8 0.9 broadcast_select_fusion.1
  57.8 96.8 %all-to-all-done = bf16[32,32,4224]{2,1,0:T(8,128)(2,1)} async-done(((bf16[32,32,4224]{2,1,0:T(8,128)(2,1)}), bf16[32,32,4224]{2,1,0:T(8,128)(2,1)}, u32[]{:S(2)}, u32[]{:S(2)}) %all-to-all-start) | async-done | bytes 8650784 | tf_op jit(solution)/shard_map/all_to_all | solution.py:101
  154.6 1.1 convert_reduce_fusion.1
  155.7 2.3 fusion.43
  158.7 4.7 %fusion.6 = bf16[256,3072]{1,0:T(8,128)(2,1)S(1)} fusion(bf16[1024,4224]{1,0:T(8,128)(2,1)} %bitcast.5, f32[1024]{0:T(1024)S(1)} %convert_reduce_fusion.1, f32[256]{0:T(256)S(1)} %rsqrt.12, f32[256]{0:T(256)S(1)} %div.51, bf16[256,1024]{1,0:T(8,128)(2,1)S(1)} %gather_fusion.3, pred[256]{0:T(512)(128)(4,1)S(1)} %compare_and_fusion.4), kind=kOutput, calls=%fused_computation.14 | convolution fusion | flops 1612972032 | bytes 8395008 | tf_op jit(solution)/shard_map/dot_general | solution.py:27
  163.5 1.0 fusion.109
  164.4 2.5 reshape.308
  167.0 1.6 reshape.310
  168.6 1.6 reshape.309
  170.3 3.2 fusion.66
  173.5 4.1 fusion.111
  177.5 5.8 %fusion.34 = bf16[8,32,16,64]{3,1,2,0:T(8,128)(2,1)} fusion(f32[8,16,32,32]{2,3,1,0:T(8,128)} %fusion.66, bf16[8,32,16,64]{3,2,1,0:T(8,128)(2,1)} %reshape.310, f32[8,16,32,32]{2,3,1,0:T(8,128)} %get-tuple-element.37, f32[8,16,32]{2,1,0:T(8,128)S(1)} %get-tuple-element.36), kind=kOutput, calls=%fused_computation.35 | convolution fusion | flops 17960992 | bytes 2113536 | tf_op jit(solution)/shard_map/ghqk,gkhd->gqhd/dot_general | solution.py:55
  183.3 5.6 %fusion.31 = bf16[8,32,16,64]{3,1,2,0:T(8,128)(2,1)} fusion(f32[8,16,32,32]{2,3,1,0:T(8,128)} %fusion.66, bf16[8,32,16,64]{3,2,1,0:T(8,128)(2,1)} %reshape.309, f32[8,16,32,32]{2,3,1,0:T(8,128)} %get-tuple-element.37, f32[8,16,32]{2,1,0:T(8,128)S(1)} %get-tuple-element.36), kind=kOutput, calls=%fused_computation.34 | convolution fusion | flops 17960992 | bytes 2113536 | tf_op jit(solution)/shard_map/ghqk,gqhd->gkhd/dot_general | solution.py:58
  188.9 3.1 fusion.30
  192.1 1.6 fusion.29
  194.1 0.7 reshape.314
  194.8 0.9 constant_dynamic-update-slice_fusion.2
  195.7 1.6 copy.66
  197.3 0.7 reshape.315
  198.0 1.6 copy.68
  199.7 0.7 reshape.316
  200.4 0.9 constant_dynamic-update-slice_fusion.1
  201.3 0.9 constant_dynamic-update-slice_fusion
  202.2 6.3 %fusion.57 = (bf16[1024]{0:T(1024)(128)(2,1)S(1)}, f32[256]{0:T(256)S(1)}, f32[256]{0:T(256)S(1)}, f32[256,1024]{1,0:T(8,128)}) fusion(f32[256]{0:T(256)S(1)} %rsqrt.12, f32[256]{0:T(256)S(1)} %div.51, bf16[256,1024]{1,0:T(8,128)(2,1)S(1)} %gather_fusion.3, pred[256]{0:T(512)(128)(4,1)S(1)} %compare_and_fusion.4, f32[1024]{0:T(1024)S(1)} %convert_reduce_fusion.1, ...), kind=kOutput, calls=%fused_computation.53 | convolution fusion | flops 1613232640 | bytes 9447680 | tf_op jit(solution)/shard_map/dot_general | solution.py:65
  208.5 4.9 %convolution_convert_fusion = bf16[1024,3072]{1,0:T(8,128)(2,1)} fusion(bf16[256,3072]{1,0:T(8,128)(2,1)S(1)} %copy-done.3, f32[1024]{0:T(1024)S(1)} %convert_reduce_fusion.1, f32[256]{0:T(256)S(1)} %rsqrt.12, f32[256]{0:T(256)S(1)} %div.51, bf16[256,1024]{1,0:T(8,128)(2,1)S(1)} %gather_fusion.3, pred[256]{0:T(512)(128)(4,1)S(1)} %compare_and_fusion.4), kind=kOutput, calls=%fused_computation.9 | convolution fusion | flops 1615331328 | bytes 8395008 | tf_op jit(solution)/shard_map/dot_general | solution.py:89
  214.6 0.7 convolution_convert_fusion.1
  215.5 6.5 %pad_maximum_fusion = bf16[1024,4224]{1,0:T(8,128)(2,1)} fusion(bf16[1024,128]{1,0:T(8,128)(2,1)S(1)} %broadcast_in_dim.181, bf16[1024,1024]{1,0:T(8,128)(2,1)S(1)} %convolution_convert_fusion.1, bf16[1024,3072]{1,0:T(8,128)(2,1)} %convolution_convert_fusion), kind=kLoop, calls=%fused_computation.8 | loop fusion | flops 25952256 | bytes 17301504 | tf_op jit(solution)/shard_map/concatenate | solution.py:161
  222.4 0.9 copy-done.5
  223.8 2.3 fusion.40
  226.8 1.2 broadcast_select_fusion
  228.0 3.6 all-to-all-start.2
  231.6 90.4 %reduce-scatter.2.cloned.1.call-done = bf16[32,4224]{1,0:T(8,128)(2,1)} async-done(((bf16[1024,4224]{1,0:T(8,128)(2,1)}), bf16[32,4224]{1,0:T(8,128)(2,1)}) %reduce-scatter.2.cloned.1.call-update) | async-done | bytes 270352 | tf_op jit(solution)/shard_map/reduce_scatter | solution.py:169
  322.1 0.9 gather_fusion.5
  323.0 0.9 gather_fusion.4
  323.8 0.9 select_bitcast_fusion
  324.7 72.4 %all-reduce.2.cloned.1.call-done = bf16[32,4224]{1,0:T(8,128)(2,1)} async-done(((bf16[32,4224]{1,0:T(8,128)(2,1)}), bf16[32,4224]{1,0:T(8,128)(2,1)}) %all-reduce.2.cloned.1.call-update) | async-done | bytes 270352 | tf_op jit(solution)/shard_map/psum | solution.py:170
  397.1 1.0 convert_element_type.105
  398.7 1.7 slice.75
  400.4 1.5 slice.76
  (80 shorter events, 7.8 us)
Async XLA Ops:
  7.2 45.1 %copy-start = (bf16[1,8,64,1024]{3,2,1,0:T(8,128)(2,1)S(1)}, bf16[1,8,64,1024]{3,2,1,0:T(8,128)(2,1)}, u32[]{:S(2)}) copy-start(bf16[1,8,64,1024]{3,2,1,0:T(8,128)(2,1)} %param.12) | copy-start | bytes 3145732
  13.5 9.4 %copy-start.11 = (bf16[32]{0:T(256)(128)(2,1)S(1)}, bf16[32]{0:T(256)(128)(2,1)}, u32[]{:S(2)}) copy-start(bf16[32]{0:T(256)(128)(2,1)} %param.18) | copy-start | bytes 196
  13.5 9.5 %copy-start.8 = (bf16[32,3072]{1,0:T(8,128)(2,1)S(1)}, bf16[32,3072]{1,0:T(8,128)(2,1)}, u32[]{:S(2)}) copy-start(bf16[32,3072]{1,0:T(8,128)(2,1)} %param.16) | copy-start | bytes 589828
  13.5 9.5 %copy-start.9 = (bf16[32,1024]{1,0:T(8,128)(2,1)S(1)}, bf16[32,1024]{1,0:T(8,128)(2,1)}, u32[]{:S(2)}) copy-start(bf16[32,1024]{1,0:T(8,128)(2,1)} %param.17) | copy-start | bytes 196612
  14.4 26.0 %all-to-all-start.1 = ((bf16[8,32,1024]{2,1,0:T(8,128)(2,1)}), bf16[8,32,1024]{2,1,0:T(8,128)(2,1)S(1)}, u32[]{:S(2)}, u32[]{:S(2)}) async-start(bf16[8,32,1024]{2,1,0:T(8,128)(2,1)} %select_select_fusion), calls=%async_computation.1 | async-start | bytes 1048576 | tf_op jit(solution)/shard_map/all_to_all | solution.py:143
  44.3 7.9 %copy-start.10 = (s32[1,8,64]{2,1,0:T(8,128)S(1)}, s32[1,8,64]{2,1,0:T(8,128)}, u32[]{:S(2)}) copy-start(s32[1,8,64]{2,1,0:T(8,128)} %param.13) | copy-start | bytes 6148
  44.3 110.3 %all-to-all-start = ((bf16[32,32,4224]{2,1,0:T(8,128)(2,1)}), bf16[32,32,4224]{2,1,0:T(8,128)(2,1)}, u32[]{:S(2)}, u32[]{:S(2)}) async-start(bf16[32,32,4224]{2,1,0:T(8,128)(2,1)} %stack.2), calls=%async_computation | async-start | bytes 17301504 | tf_op jit(solution)/shard_map/all_to_all | solution.py:101
  52.1 269.9 %reduce-scatter.2.cloned.1.call-start = ((), (), s32[]{:S(2)}) async-start(), calls=%async_computation.4 | async-start | bytes 8921088 | tf_op jit(solution)/shard_map/reduce_scatter | solution.py:169
  188.9 3.2 copy-start.2
  188.9 3.2 copy-start.12
  192.1 1.6 copy-start.7
  202.2 6.3 %copy-start.3 = (bf16[256,3072]{1,0:T(8,128)(2,1)S(1)}, bf16[256,3072]{1,0:T(8,128)(2,1)}, u32[]{:S(2)}) copy-start(bf16[256,3072]{1,0:T(8,128)(2,1)} %constant_dynamic-update-slice_fusion) | copy-start | bytes 4718596
  208.5 4.9 %copy-start.6 = (bf16[8,32,16,64]{3,1,2,0:T(8,128)(2,1)S(1)}, bf16[8,32,16,64]{3,1,2,0:T(8,128)(2,1)}, u32[]{:S(2)}) copy-start(bf16[8,32,16,64]{3,1,2,0:T(8,128)(2,1)} %fusion.29) | copy-start | bytes 1572868
  213.4 1.1 copy-start.4
  222.1 1.2 copy-start.5
  228.0 94.0 %all-to-all-start.2 = ((bf16[8,32,2048]{2,1,0:T(8,128)(2,1)}), bf16[8,32,2048]{2,1,0:T(8,128)(2,1)S(1)}, u32[]{:S(2)}, u32[]{:S(2)}) async-start(bf16[8,32,2048]{2,1,0:T(8,128)(2,1)} %broadcast_select_fusion), calls=%async_computation.2 | async-start | bytes 2097152 | tf_op jit(solution)/shard_map/all_to_all | solution.py:150
  231.5 165.6 %all-reduce.2.cloned.1.call-start = ((), (), s32[]{:S(2)}) async-start(), calls=%async_computation.5 | async-start | bytes 540672 | tf_op jit(solution)/shard_map/psum | solution.py:170
  322.9 79.0 %copy-start.1 = (bf16[1,8,64,1024]{3,2,1,0:T(8,128)(2,1)S(1)}, bf16[1,8,64,1024]{3,2,1,0:T(8,128)(2,1)}, u32[]{:S(2)}) copy-start(bf16[1,8,64,1024]{3,2,1,0:T(8,128)(2,1)} %param.12) | copy-start | bytes 3145732
Sparse Core Ops, SparseCore 0:
  222.2 99.6 reduce-scatter.1
  324.3 72.7 all-reduce.1
